TPU v7x, 32 devices: a whole 2x2x4 slice. The times are simulated.
32 devices in a mesh: wave: 4 (over z), lev: 8 (over y, x, core).
Axes of the slice: x: 2, y: 2, z: 4, core: 2. Of those that a mesh axis runs over, the one named last changes fastest.
Arguments:
- spec: bfloat16 [1280, 2, 16, 1280], P('wave', None, 'lev'), may hold values from -0.119628906 to 0.119628906
- legendre: bfloat16 [1280, 16, 1280], P(('wave', 'lev')), may hold values from -0.15625 to 0.15625
- slot_wave: int32 [1280], replicated, may hold values from 0 to 1280, as said below
- row_lons: int32 [32], replicated, may hold values from 20 to 5136, as said below
- band_rows: int32 [32], replicated, may hold values from 0 to 31, as said below
Outputs:
- grid: float32 [32, 16, 5136], P('wave', 'lev')
Inputs may be any that keep to these rules, and one draw needn't show every extreme that they name: `slot_wave`: every zonal wavenumber 0 to 1279 stands in exactly one slot; any other slot holds 1280. `row_lons`: row 16 + j has as many points as row j; each count is 20 plus a multiple of 4; some row has 5136. `band_rows`: a permutation of the latitude rows.
All inputs are finite; a program needn't handle non-finite values.
Results may differ from a plain program's by a relative error of at most 0.0037.
Values may be sent and summed in bfloat16 or wider, within the bound.
No kernel may reach another device: no remote copies, remote signals or barrier semaphores. Data moves between devices by JAX's collectives and lax.ppermute only.
A program may use at most 64 MiB of HBM per device.

v0:
```python
import math
import jax
import jax.numpy as jnp
import numpy as np
from jax import lax
from jax.sharding import Mesh
from jax.sharding import PartitionSpec as P


def angles(remainder, points):
    return 2.0 * math.pi * remainder.astype(jnp.float32) / points.astype(jnp.float32)


def trig_pair(step, lon_idx, points, count):
    mult = jnp.arange(count, dtype=jnp.int32)[:, None] * step
    theta = angles(mult * lon_idx[None, :] % points, points)
    return (jnp.cos(theta), jnp.sin(theta))


def compose(first, second):
    c0, s0 = first
    c1, s1 = second
    cos = c1[:, None] * c0[None] - s1[:, None] * s0[None]
    sin = s1[:, None] * c0[None] + c1[:, None] * s0[None]
    return (cos.reshape(-1, cos.shape[-1]), sin.reshape(-1, sin.shape[-1]))


def row_synthesis(coef_row, points):
    fields = coef_row.shape[1]
    waves = coef_row.shape[2]
    ablocks = waves // 64
    lon_len = 20 + 4 * (waves - 1)
    lon_idx = jnp.arange(lon_len, dtype=jnp.int32)
    cos_t, sin_t = compose(trig_pair(1, lon_idx, points, 8), trig_pair(8, lon_idx, points, 8))
    cosb = cos_t.astype(jnp.bfloat16)
    sinb = sin_t.astype(jnp.bfloat16)
    n_a1 = -(-ablocks // 4)
    cosp, sinp = compose(trig_pair(64, lon_idx, points, 4), trig_pair(256, lon_idx, points, n_a1))
    cosp = cosp[:ablocks]
    sinp = sinp[:ablocks]
    blocks = coef_row.reshape(2, fields, ablocks, 64)
    c0 = blocks[0]
    c1 = blocks[1]
    lhs = jnp.stack([jnp.concatenate([c0, -c1], -1), jnp.concatenate([c1, c0], -1)], 0)
    rhs = jnp.concatenate([cosb, sinb], 0)
    part = jnp.einsum("dfab,bi->dfai", lhs, rhs, preferred_element_type=jnp.float32)
    total = jnp.sum(part[0] * cosp[None] - part[1] * sinp[None], axis=1)
    return jnp.where(lon_idx[None, :] < points, total, jnp.zeros_like(total))


def on_device(spec, legendre, slot_wave, row_lons, band_rows, rows_per_dev):
    n_wave = lax.axis_size("wave")
    n_g = lax.axis_size("lev_g")
    n_r = lax.axis_size("lev_r")
    n_lev = n_g * n_r
    per_dev = legendre.shape[0]
    nlath = legendre.shape[1]
    waves = spec.shape[-1]
    trunc_top = waves - 1
    lev_idx = lax.axis_index("lev_g") * n_r + lax.axis_index("lev_r")
    spec_v = spec.reshape((n_lev, per_dev) + spec.shape[1:])
    gathered = lax.all_to_all(spec_v, ("lev_g", "lev_r"), split_axis=0, concat_axis=0, tiled=True)
    fields = gathered.shape[3] * n_lev
    first_slot = (lax.axis_index("wave") * n_lev + lev_idx) * per_dev
    my_waves = lax.dynamic_slice_in_dim(slot_wave, first_slot, per_dev)
    degree = jnp.arange(waves, dtype=jnp.int32)
    live_k = degree[None, :] <= trunc_top - my_waves[:, None]
    even_mask = (live_k & (degree[None, :] % 2 == 0))[:, None, :]
    odd_mask = (live_k & (degree[None, :] % 2 == 1))[:, None, :]
    zeros = jnp.zeros_like(legendre)
    leg2 = jnp.concatenate(
        [jnp.where(even_mask, legendre, zeros), jnp.where(odd_mask, legendre, zeros)], 1
    )
    sums = jnp.einsum("lscfk,sjk->sclfj", gathered, leg2, preferred_element_type=jnp.float32)
    sums = sums.reshape(per_dev, 2, fields, 2 * nlath)
    north = band_rows < nlath
    lat_idx = jnp.where(north, band_rows, band_rows - nlath)
    j2 = jnp.arange(2 * nlath, dtype=jnp.int32)[:, None]
    sel = jnp.where(j2 == lat_idx[None, :], 1.0, 0.0) + jnp.where(
        j2 == nlath + lat_idx[None, :], jnp.where(north, 1.0, -1.0)[None, :], 0.0
    )
    fourier = jnp.einsum(
        "scfj,jp->scfp",
        sums,
        sel,
        precision=lax.Precision.HIGHEST,
        preferred_element_type=jnp.float32,
    ).astype(jnp.bfloat16)
    rows = band_rows.shape[0]
    fpg = fields // n_g
    fourier = fourier.reshape(per_dev, 2, n_g, fpg, n_wave, n_r, rows_per_dev)
    fourier = jnp.transpose(fourier, (4, 2, 5, 1, 3, 6, 0))
    fourier = fourier.reshape(n_wave * n_g * n_r, 2, fpg, rows_per_dev, per_dev)
    banded = lax.all_to_all(
        fourier, ("wave", "lev_g", "lev_r"), split_axis=0, concat_axis=0, tiled=True
    )
    banded = jnp.transpose(banded, (1, 2, 3, 0, 4)).reshape(2, fpg, rows_per_dev, -1)
    wave_idx = jnp.arange(waves, dtype=jnp.int32)
    first_row = (lax.axis_index("wave") * n_r + lax.axis_index("lev_r")) * rows_per_dev
    my_rows = lax.dynamic_slice_in_dim(band_rows, first_row, rows_per_dev)
    row_points = row_lons[my_rows]
    keep = 2 * wave_idx[None, :] < row_points[:, None]
    factor = jnp.where(keep, jnp.where(wave_idx[None, :] == 0, 2.0, 4.0), 0.0) / 2.0
    onehot = jnp.where(
        slot_wave[None, :, None] == wave_idx[None, None, :], factor[:, None, :], 0.0
    ).astype(jnp.bfloat16)
    coef = jnp.einsum("cfrs,rsm->cfrm", banded, onehot, preferred_element_type=jnp.float32)
    coef = coef.astype(jnp.bfloat16)
    coef_rows = jnp.moveaxis(coef, 2, 0)
    if rows_per_dev == 1:
        grid = row_synthesis(coef_rows[0], row_points[0])[None]
    else:
        grid = lax.map(lambda item: row_synthesis(item[0], item[1]), (coef_rows, row_points))
    lon = grid.shape[-1]
    fpd = fpg // n_r
    grid = grid.reshape(rows_per_dev, n_r, fpd, lon)
    grid = lax.all_to_all(grid, "lev_r", split_axis=1, concat_axis=0, tiled=True)
    return grid.reshape(n_r * rows_per_dev, fpd, lon)


def solution(mesh):

    def run(spec, legendre, slot_wave, row_lons, band_rows):
        n_wave = mesh.shape["wave"]
        n_lev = mesh.shape["lev"]
        rows_w = band_rows.shape[0] // n_wave
        if n_lev >= rows_w:
            n_r = rows_w
            rows_per_dev = 1
        else:
            n_r = n_lev
            rows_per_dev = rows_w // n_lev
        n_g = n_lev // n_r
        devs = np.asarray(mesh.devices).reshape(n_wave, n_g, n_r)
        mesh2 = Mesh(devs, ("wave", "lev_g", "lev_r"))
        lev = ("lev_g", "lev_r")
        fn = jax.shard_map(
            lambda *a: on_device(*a, rows_per_dev=rows_per_dev),
            mesh=mesh2,
            in_specs=(P("wave", None, lev, None), P(("wave",) + lev, None, None), P(), P(), P()),
            out_specs=P("wave", lev, None),
            check_vma=False,
        )
        return fn(spec, legendre, slot_wave, row_lons, band_rows)

    return run
```

profile of v0, /device:TPU:0, one launch (start us, length us, event | category | flops | bytes accessed | tf_op | source)
XLA Modules:
  0.0 82.8 jit_solution(6043936887507259313)
XLA Ops:
  0.0 0.0 copy-start.11
  0.0 0.0 copy-start.10
  0.0 5.3 %all-to-all-start = ((bf16[8,40,2,2,1280]{4,3,2,1,0:T(2,128)(2,1)}), bf16[8,40,2,2,1280]{4,3,2,1,0:T(2,128)(2,1)S(1)}, u32[]{:S(2)}, u32[]{:S(2)}) async-start(bf16[8,40,2,2,1280]{4,3,2,1,0:T(2,128)(2,1)} %bitcast.81), calls=%async_computation | async-start | bytes 6553600 | tf_op jit(solution)/shard_map/all_to_all | solution.py:62
  5.3 0.0 copy-done.11
  5.4 0.6 dynamic_slice.6
  7.9 0.0 copy-done.10
  7.9 0.6 dynamic-slice.2
  10.4 2.9 %fusion.61 = (f32[8,5136]{1,0:T(8,128)S(1)}, f32[8,5136]{1,0:T(8,128)}) fusion(f32[]{:T(128)S(6)} %convert_element_type.83, pred[]{:T(512)S(6)} %lt.109, s32[]{:T(128)S(6)} %select_n.155), kind=kLoop, calls=%fused_computation.79 | loop fusion | flops 451968 | bytes 328713 | tf_op jit(solution)/shard_map/sin | solution.py:17
  13.4 3.1 %fusion.64 = (f32[8,5136]{1,0:T(8,128)}, f32[8,5136]{1,0:T(8,128)}) fusion(f32[]{:T(128)S(6)} %convert_element_type.83, pred[]{:T(512)S(6)} %lt.109, s32[]{:T(128)S(6)} %select_n.155, s32[8]{0:T(128)S(1)} %iota_multiply_fusion.2), kind=kLoop, calls=%fused_computation.82 | loop fusion | flops 451968 | bytes 328745 | tf_op jit(solution)/shard_map/cos | solution.py:17
  16.4 3.0 %fusion.60 = (f32[5,5136]{1,0:T(8,128)}, f32[5,5136]{1,0:T(8,128)}) fusion(f32[]{:T(128)S(6)} %convert_element_type.83, pred[]{:T(512)S(6)} %lt.109, s32[]{:T(128)S(6)} %select_n.155, s32[5]{0:T(128)S(1)} %iota_multiply_fusion.1), kind=kLoop, calls=%fused_computation.78 | loop fusion | flops 282480 | bytes 205469 | tf_op jit(solution)/shard_map/cos | solution.py:17
  19.5 3.0 %fusion.66 = (f32[4,5136]{1,0:T(4,128)S(1)}, f32[4,5136]{1,0:T(4,128)}) fusion(f32[]{:T(128)S(6)} %convert_element_type.83, pred[]{:T(512)S(6)} %lt.109, s32[]{:T(128)S(6)} %select_n.155, s32[4]{0:T(128)S(1)} %iota_multiply_fusion), kind=kLoop, calls=%fused_computation.84 | loop fusion | flops 225984 | bytes 164377 | tf_op jit(solution)/shard_map/cos | solution.py:17
  22.4 0.0 copy-start.6
  22.4 0.0 copy-start.7
  22.4 0.0 copy-start.8
  22.4 0.8 dynamic-slice_subtract_fusion
  23.3 0.1 fusion.27
  23.4 0.0 copy-start.3
  23.4 0.0 copy-start.4
  23.4 0.0 copy-start.5
  23.4 3.6 %broadcast_select_fusion.1 = (bf16[40,16,1280]{2,1,0:T(8,128)(2,1)}, bf16[40,16,1280]{2,1,0:T(8,128)(2,1)}) fusion(bf16[40,16,1280]{2,1,0:T(8,128)(2,1)} %param.6, pred[40,1280]{1,0:T(8,128)(4,1)S(1)} %get-tuple-element.32, pred[40,1280]{1,0:T(8,128)(4,1)S(1)} %get-tuple-element.33), kind=kLoop, calls=%fused_computation.18 | loop fusion | flops 1638400 | bytes 5017600 | tf_op jit(solution)/shard_map/jit(_where)/select_n | solution.py:72
  27.1 0.0 copy-done.6
  27.1 0.0 copy-done.7
  27.1 0.0 copy-done.8
  27.1 1.1 %multiply_subtract_fusion = (f32[5,4,5136]{2,1,0:T(4,128)}, f32[5,4,5136]{2,1,0:T(4,128)}) fusion(f32[4,5136]{1,0:T(4,128)S(1)} %copy-done.8, f32[5,5136]{1,0:T(8,128)S(1)} %copy-done.7, f32[4,5136]{1,0:T(4,128)S(1)} %get-tuple-element.28, f32[5,5136]{1,0:T(8,128)S(1)} %copy-done.6), kind=kLoop, calls=%fused_computation.31 | loop fusion | flops 616320 | bytes 1191552 | tf_op jit(solution)/shard_map/sub | solution.py:23
  28.2 0.0 copy-done.3
  28.2 0.0 copy-done.4
  28.2 0.0 copy-done.5
  28.2 1.4 %fusion.24 = (bf16[64,5136]{1,0:T(8,128)(2,1)}, bf16[64,5136]{1,0:T(8,128)(2,1)}) fusion(f32[8,5136]{1,0:T(8,128)S(1)} %get-tuple-element.36, f32[8,5136]{1,0:T(8,128)S(1)} %copy-done.5, f32[8,5136]{1,0:T(8,128)S(1)} %copy-done.3, f32[8,5136]{1,0:T(8,128)S(1)} %copy-done.4), kind=kLoop, calls=%fused_computation.28 | loop fusion | flops 2629632 | bytes 1972224 | tf_op jit(solution)/shard_map/convert_element_type | solution.py:35
  29.6 15.0 %all-to-all-done = bf16[8,40,2,2,1280]{4,3,2,1,0:T(2,128)(2,1)S(1)} async-done(((bf16[8,40,2,2,1280]{4,3,2,1,0:T(2,128)(2,1)}), bf16[8,40,2,2,1280]{4,3,2,1,0:T(2,128)(2,1)S(1)}, u32[]{:S(2)}, u32[]{:S(2)}) %all-to-all-start) | async-done | bytes 3276832 | tf_op jit(solution)/shard_map/all_to_all | solution.py:62
  44.6 5.0 %fusion.20 = f32[40,2,8,2,32]{4,2,3,1,0:T(8,128)} fusion(bf16[8,40,2,2,1280]{4,3,2,1,0:T(2,128)(2,1)S(1)} %all-to-all-done, bf16[40,16,1280]{2,1,0:T(8,128)(2,1)} %get-tuple-element.17, bf16[40,16,1280]{2,1,0:T(8,128)(2,1)} %get-tuple-element.16), kind=kOutput, calls=%fused_computation.25 | convolution fusion | flops 111411200 | bytes 6717440 | tf_op jit(solution)/shard_map/lscfk,sjk->sclfj/dot_general | solution.py:74
  49.6 0.0 copy-start.1
  49.6 0.0 copy-start
  49.6 1.5 %copy.14 = f32[40,2,8,2,32]{0,4,3,2,1:T(8,128)S(1)} copy(f32[40,2,8,2,32]{4,2,3,1,0:T(8,128)} %fusion.20) | data formatting | bytes 327680 | tf_op jit(solution)/shard_map/lscfk,sjk->sclfj/transpose | solution.py:74
  51.1 0.6 fusion.23
  51.7 0.1 copy.15
  51.9 1.0 %reshape.476 = bf16[32,2,640]{2,1,0:T(2,128)(2,1)} reshape(bf16[32,1,2,16,40]{4,3,2,1,0:T(8,128)(2,1)S(1)} %bitcast.84) | data formatting | bytes 163840
  52.9 4.0 %all-to-all-start.1 = ((bf16[32,2,640]{2,1,0:T(2,128)(2,1)}), bf16[32,2,640]{2,1,0:T(2,128)(2,1)S(1)}, u32[]{:S(2)}, u32[]{:S(2)}) async-start(bf16[32,2,640]{2,1,0:T(2,128)(2,1)} %reshape.476), calls=%async_computation.1 | async-start | bytes 163840 | tf_op jit(solution)/shard_map/all_to_all | solution.py:94
  56.9 0.6 select_multiply_fusion
  57.5 0.0 copy-done.1
  57.5 1.3 %copy.17 = bf16[64,5136]{0,1:T(8,128)(2,1)S(1)} copy(bf16[64,5136]{1,0:T(8,128)(2,1)S(1)} %copy-done.1) | data formatting | bytes 1314816 | tf_op jit(solution)/shard_map/convert_element_type | solution.py:35
  58.8 0.0 copy-done
  58.9 0.0 copy-start.9
  58.9 1.3 %copy.18 = bf16[64,5136]{0,1:T(8,128)(2,1)S(1)} copy(bf16[64,5136]{1,0:T(8,128)(2,1)S(1)} %copy-done) | data formatting | bytes 1314816 | tf_op jit(solution)/shard_map/convert_element_type | solution.py:36
  60.2 1.2 %add.119 = f32[20,5136]{1,0:T(8,128)S(1)} reshape(f32[5,4,5136]{2,1,0:T(4,128)} %get-tuple-element.21) | data formatting | bytes 821760 | tf_op jit(solution)/shard_map/add | solution.py:24
  61.3 2.0 %sub.33 = f32[20,5136]{1,0:T(8,128)} reshape(f32[5,4,5136]{2,1,0:T(4,128)} %get-tuple-element.20) | data formatting | bytes 821760 | tf_op jit(solution)/shard_map/sub | solution.py:23
  63.3 0.6 iota_compare_fusion.2
  63.9 0.5 all-to-all-done.1
  64.5 0.4 reshape.477
  64.9 0.1 copy.16
  65.0 0.3 reshape.449
  65.3 0.0 copy-done.9
  65.4 0.7 fusion.14
  66.1 0.1 squeeze.17
  66.3 0.1 squeeze.16
  66.4 0.1 maximum_bitcast_fusion.6
  66.5 0.0 copy-start.2
  66.5 2.4 %fusion.17 = f32[2,16,20,5136]{3,2,1,0:T(8,128)S(1)} fusion(bf16[64,5136]{0,1:T(8,128)(2,1)S(1)} %copy.18, bf16[64,5136]{0,1:T(8,128)(2,1)S(1)} %copy.17, bf16[1,16,20,128]{3,2,1,0:T(8,128)(2,1)S(1)} %get-tuple-element.23, bf16[1,16,20,128]{3,2,1,0:T(8,128)(2,1)S(1)} %get-tuple-element.22), kind=kOutput, calls=%fused_computation.22 | convolution fusion | flops 844193792 | bytes 14626816 | tf_op jit(solution)/shard_map/dfab,bi->dfai/dot_general | solution.py:46
  69.0 0.0 copy-done.2
  69.0 1.8 %fusion.2 = f32[16,5136]{1,0:T(8,128)S(1)} fusion(f32[2,16,20,5136]{3,2,1,0:T(8,128)S(1)} %fusion.17, f32[20,5136]{1,0:T(8,128)S(1)} %add.119, f32[20,5136]{1,0:T(8,128)S(1)} %copy-done.2), kind=kLoop, calls=%fused_computation.3 | loop fusion | flops 6491904 | bytes 14298624 | tf_op jit(solution)/shard_map/reduce_sum | solution.py:47
  70.8 0.2 reduce_sum.12
  71.0 0.2 broadcast_select_fusion.2
  71.1 10.9 %all_to_all.19 = f32[1,8,2,5136]{3,2,0,1:T(2,128)S(1)} all-to-all(f32[1,8,2,5136]{3,2,0,1:T(2,128)S(1)} %broadcast_select_fusion.2), channel_id=1, replica_groups=mesh['wave'=4,'lev'=8] {'lev'}, dimensions={1} | all-to-all | bytes 657408 | tf_op jit(solution)/shard_map/all_to_all | solution.py:117
  82.1 0.7 copy.28
  (9 shorter events, 0.1 us)
Async XLA Ops:
  0.0 5.3 %copy-start.11 = (s32[32]{0:T(128)S(1)}, s32[32]{0:T(128)}, u32[]{:S(2)}) copy-start(s32[32]{0:T(128)} %param.9) | copy-start | bytes 388
  0.0 7.9 %copy-start.10 = (s32[32]{0:T(128)S(1)}, s32[32]{0:T(128)}, u32[]{:S(2)}) copy-start(s32[32]{0:T(128)} %param.8) | copy-start | bytes 388
  0.0 44.6 %all-to-all-start = ((bf16[8,40,2,2,1280]{4,3,2,1,0:T(2,128)(2,1)}), bf16[8,40,2,2,1280]{4,3,2,1,0:T(2,128)(2,1)S(1)}, u32[]{:S(2)}, u32[]{:S(2)}) async-start(bf16[8,40,2,2,1280]{4,3,2,1,0:T(2,128)(2,1)} %bitcast.81), calls=%async_computation | async-start | bytes 6553600 | tf_op jit(solution)/shard_map/all_to_all | solution.py:62
  22.4 4.6 %copy-start.6 = (f32[5,5136]{1,0:T(8,128)S(1)}, f32[5,5136]{1,0:T(8,128)}, u32[]{:S(2)}) copy-start(f32[5,5136]{1,0:T(8,128)} %get-tuple-element.26) | copy-start | bytes 308164
  22.4 4.6 %copy-start.7 = (f32[5,5136]{1,0:T(8,128)S(1)}, f32[5,5136]{1,0:T(8,128)}, u32[]{:S(2)}) copy-start(f32[5,5136]{1,0:T(8,128)} %get-tuple-element.27) | copy-start | bytes 308164
  22.4 4.6 %copy-start.8 = (f32[4,5136]{1,0:T(4,128)S(1)}, f32[4,5136]{1,0:T(4,128)}, u32[]{:S(2)}) copy-start(f32[4,5136]{1,0:T(4,128)} %get-tuple-element.29) | copy-start | bytes 246532
  23.4 4.8 %copy-start.3 = (f32[8,5136]{1,0:T(8,128)S(1)}, f32[8,5136]{1,0:T(8,128)}, u32[]{:S(2)}) copy-start(f32[8,5136]{1,0:T(8,128)} %get-tuple-element.37) | copy-start | bytes 493060
  23.4 4.8 %copy-start.4 = (f32[8,5136]{1,0:T(8,128)S(1)}, f32[8,5136]{1,0:T(8,128)}, u32[]{:S(2)}) copy-start(f32[8,5136]{1,0:T(8,128)} %get-tuple-element.34) | copy-start | bytes 493060
  23.4 4.8 %copy-start.5 = (f32[8,5136]{1,0:T(8,128)S(1)}, f32[8,5136]{1,0:T(8,128)}, u32[]{:S(2)}) copy-start(f32[8,5136]{1,0:T(8,128)} %get-tuple-element.35) | copy-start | bytes 493060
  49.6 7.9 %copy-start.1 = (bf16[64,5136]{1,0:T(8,128)(2,1)S(1)}, bf16[64,5136]{1,0:T(8,128)(2,1)}, u32[]{:S(2)}) copy-start(bf16[64,5136]{1,0:T(8,128)(2,1)} %get-tuple-element.18) | copy-start | bytes 1972228
  49.6 9.3 %copy-start = (bf16[64,5136]{1,0:T(8,128)(2,1)S(1)}, bf16[64,5136]{1,0:T(8,128)(2,1)}, u32[]{:S(2)}) copy-start(bf16[64,5136]{1,0:T(8,128)(2,1)} %get-tuple-element.19) | copy-start | bytes 1972228
  52.9 11.6 %all-to-all-start.1 = ((bf16[32,2,640]{2,1,0:T(2,128)(2,1)}), bf16[32,2,640]{2,1,0:T(2,128)(2,1)S(1)}, u32[]{:S(2)}, u32[]{:S(2)}) async-start(bf16[32,2,640]{2,1,0:T(2,128)(2,1)} %reshape.476), calls=%async_computation.1 | async-start | bytes 163840 | tf_op jit(solution)/shard_map/all_to_all | solution.py:94
  58.9 6.5 %copy-start.9 = (s32[1280]{0:T(1024)S(1)}, s32[1280]{0:T(1024)}, u32[]{:S(2)}) copy-start(s32[1280]{0:T(1024)} %param.7) | copy-start | bytes 15364
  66.5 2.4 %copy-start.2 = (f32[20,5136]{1,0:T(8,128)S(1)}, f32[20,5136]{1,0:T(8,128)}, u32[]{:S(2)}) copy-start(f32[20,5136]{1,0:T(8,128)} %sub.33) | copy-start | bytes 1232644
where the time goes:
time: 83.3 us; the launch traced here: 82.8 us
  other arithmetic  22.5 us (27%)
  waiting for transfers between devices  15.5 us (19%)
  local copies, waits for them, and re-layouts  11.6 us (14%)
  blocking collectives  10.9 us (13%)
  starting transfers between devices  9.3 us (11%)
  matrix products  8.76 us (11%)
  between operations  4.15 us (5%)
    all_to_all x1, waiting for transfers between devices, on_device(): lax.all_to_all(spec_v, ('lev_g', 'lev_r'), split_axis=0, concat_axis=0, t...  15 us
    all_to_all x1, blocking collectives, on_device(): lax.all_to_all(grid, 'lev_r', split_axis=1, concat_axis=0, tiled=True)  10.9 us
    cos x3, other arithmetic, trig_pair(): return (jnp.cos(theta), jnp.sin(theta))  9.06 us
    all_to_all x1, starting transfers between devices, on_device(): lax.all_to_all(spec_v, ('lev_g', 'lev_r'), split_axis=0, concat_axis=0, t...  5.3 us
    dot_general x1, matrix products, on_device(): jnp.einsum('lscfk,sjk->sclfj', gathered, leg2, preferred_element_type=jnp...  4.99 us
    all_to_all x1, starting transfers between devices, on_device(): lax.all_to_all(fourier, ('wave', 'lev_g', 'lev_r'), split_axis=0, concat_...  4 us
    select_n x1, other arithmetic, on_device(): jnp.where(even_mask, legendre, zeros)  3.64 us
    sin x1, other arithmetic, trig_pair(): return (jnp.cos(theta), jnp.sin(theta))  2.94 us
  transfers between devices with their start and end apart: 2, of which 2 were waited for; matrix products, arithmetic and copies ran while one was open for 33% of the time, Pallas kernels for 0%

commit v1 on v0

--- a/solution.py
+++ b/solution.py
@@ -114,7 +114,10 @@
     lon = grid.shape[-1]
     fpd = fpg // n_r
     grid = grid.reshape(rows_per_dev, n_r, fpd, lon)
-    grid = lax.all_to_all(grid, "lev_r", split_axis=1, concat_axis=0, tiled=True)
+    grid = jnp.concatenate(
+        lax.all_to_all(jnp.stack(jnp.split(grid, lax.axis_size("lev_r"), axis=1)), "lev_r", 0, 0),
+        axis=0,
+    )
     return grid.reshape(n_r * rows_per_dev, fpd, lon)
 
 

time: 83.3 us -> 83.4 us (level)
    unnamed x27 -> x34, local copies, waits for them, and re-layouts: 2.18 us -> 2.25 us
where the time goes in v1:
time: 83.4 us; the launch traced here: 82.9 us
  other arithmetic  22.5 us (27%)
  waiting for transfers between devices  15.5 us (19%)
  local copies, waits for them, and re-layouts  11.7 us (14%)
  blocking collectives  10.9 us (13%)
  starting transfers between devices  9.3 us (11%)
  matrix products  8.76 us (11%)
  between operations  4.2 us (5%)
    all_to_all x1, waiting for transfers between devices, on_device(): lax.all_to_all(spec_v, ('lev_g', 'lev_r'), split_axis=0, concat_axis=0, t...  15 us
    all_to_all x1, blocking collectives, on_device(): lax.all_to_all(jnp.stack(jnp.split(grid, lax.axis_size('lev_r'), axis=1))...  10.9 us
    cos x3, other arithmetic, trig_pair(): return (jnp.cos(theta), jnp.sin(theta))  9.06 us
    all_to_all x1, starting transfers between devices, on_device(): lax.all_to_all(spec_v, ('lev_g', 'lev_r'), split_axis=0, concat_axis=0, t...  5.3 us
    dot_general x1, matrix products, on_device(): jnp.einsum('lscfk,sjk->sclfj', gathered, leg2, preferred_element_type=jnp...  4.99 us
    all_to_all x1, starting transfers between devices, on_device(): lax.all_to_all(fourier, ('wave', 'lev_g', 'lev_r'), split_axis=0, concat_...  4 us
    select_n x1, other arithmetic, on_device(): jnp.where(even_mask, legendre, zeros)  3.64 us
    sin x1, other arithmetic, trig_pair(): return (jnp.cos(theta), jnp.sin(theta))  2.94 us
  transfers between devices with their start and end apart: 2, of which 2 were waited for; matrix products, arithmetic and copies ran while one was open for 33% of the time, Pallas kernels for 0%

profile of v1, /device:TPU:0, one launch (start us, length us, event | category | flops | bytes accessed | tf_op | source)
XLA Modules:
  0.0 82.9 jit_solution(17707785176414112282)
XLA Ops:
  0.0 0.0 copy-start.11
  0.0 0.0 copy-start.10
  0.0 5.3 %all-to-all-start = ((bf16[8,40,2,2,1280]{4,3,2,1,0:T(2,128)(2,1)}), bf16[8,40,2,2,1280]{4,3,2,1,0:T(2,128)(2,1)S(1)}, u32[]{:S(2)}, u32[]{:S(2)}) async-start(bf16[8,40,2,2,1280]{4,3,2,1,0:T(2,128)(2,1)} %bitcast.113), calls=%async_computation | async-start | bytes 6553600 | tf_op jit(solution)/shard_map/all_to_all | solution.py:62
  5.3 0.0 copy-done.11
  5.4 0.6 dynamic_slice.6
  7.9 0.0 copy-done.10
  7.9 0.6 dynamic-slice.2
  10.4 2.9 %fusion.61 = (f32[8,5136]{1,0:T(8,128)S(1)}, f32[8,5136]{1,0:T(8,128)}) fusion(f32[]{:T(128)S(6)} %convert_element_type.83, pred[]{:T(512)S(6)} %lt.109, s32[]{:T(128)S(6)} %select_n.155), kind=kLoop, calls=%fused_computation.79 | loop fusion | flops 451968 | bytes 328713 | tf_op jit(solution)/shard_map/sin | solution.py:17
  13.4 3.1 %fusion.64 = (f32[8,5136]{1,0:T(8,128)}, f32[8,5136]{1,0:T(8,128)}) fusion(f32[]{:T(128)S(6)} %convert_element_type.83, pred[]{:T(512)S(6)} %lt.109, s32[]{:T(128)S(6)} %select_n.155, s32[8]{0:T(128)S(1)} %iota_multiply_fusion.2), kind=kLoop, calls=%fused_computation.82 | loop fusion | flops 451968 | bytes 328745 | tf_op jit(solution)/shard_map/cos | solution.py:17
  16.4 3.0 %fusion.60 = (f32[5,5136]{1,0:T(8,128)}, f32[5,5136]{1,0:T(8,128)}) fusion(f32[]{:T(128)S(6)} %convert_element_type.83, pred[]{:T(512)S(6)} %lt.109, s32[]{:T(128)S(6)} %select_n.155, s32[5]{0:T(128)S(1)} %iota_multiply_fusion.1), kind=kLoop, calls=%fused_computation.78 | loop fusion | flops 282480 | bytes 205469 | tf_op jit(solution)/shard_map/cos | solution.py:17
  19.5 3.0 %fusion.74 = (f32[4,5136]{1,0:T(4,128)S(1)}, f32[4,5136]{1,0:T(4,128)}) fusion(f32[]{:T(128)S(6)} %convert_element_type.83, pred[]{:T(512)S(6)} %lt.109, s32[]{:T(128)S(6)} %select_n.155, s32[4]{0:T(128)S(1)} %iota_multiply_fusion), kind=kLoop, calls=%fused_computation.100 | loop fusion | flops 225984 | bytes 164377 | tf_op jit(solution)/shard_map/cos | solution.py:17
  22.4 0.0 copy-start.6
  22.4 0.0 copy-start.7
  22.4 0.0 copy-start.8
  22.4 0.8 dynamic-slice_subtract_fusion
  23.3 0.1 fusion.27
  23.4 0.0 copy-start.3
  23.4 0.0 copy-start.4
  23.4 0.0 copy-start.5
  23.4 3.6 %broadcast_select_fusion.1 = (bf16[40,16,1280]{2,1,0:T(8,128)(2,1)}, bf16[40,16,1280]{2,1,0:T(8,128)(2,1)}) fusion(bf16[40,16,1280]{2,1,0:T(8,128)(2,1)} %param.6, pred[40,1280]{1,0:T(8,128)(4,1)S(1)} %get-tuple-element.32, pred[40,1280]{1,0:T(8,128)(4,1)S(1)} %get-tuple-element.33), kind=kLoop, calls=%fused_computation.18 | loop fusion | flops 1638400 | bytes 5017600 | tf_op jit(solution)/shard_map/jit(_where)/select_n | solution.py:72
  27.1 0.0 copy-done.6
  27.1 0.0 copy-done.7
  27.1 0.0 copy-done.8
  27.1 1.1 %multiply_subtract_fusion = (f32[5,4,5136]{2,1,0:T(4,128)}, f32[5,4,5136]{2,1,0:T(4,128)}) fusion(f32[4,5136]{1,0:T(4,128)S(1)} %copy-done.8, f32[5,5136]{1,0:T(8,128)S(1)} %copy-done.7, f32[4,5136]{1,0:T(4,128)S(1)} %get-tuple-element.28, f32[5,5136]{1,0:T(8,128)S(1)} %copy-done.6), kind=kLoop, calls=%fused_computation.31 | loop fusion | flops 616320 | bytes 1191552 | tf_op jit(solution)/shard_map/sub | solution.py:23
  28.2 0.0 copy-done.3
  28.2 0.0 copy-done.4
  28.2 0.0 copy-done.5
  28.2 1.4 %fusion.24 = (bf16[64,5136]{1,0:T(8,128)(2,1)}, bf16[64,5136]{1,0:T(8,128)(2,1)}) fusion(f32[8,5136]{1,0:T(8,128)S(1)} %get-tuple-element.36, f32[8,5136]{1,0:T(8,128)S(1)} %copy-done.5, f32[8,5136]{1,0:T(8,128)S(1)} %copy-done.3, f32[8,5136]{1,0:T(8,128)S(1)} %copy-done.4), kind=kLoop, calls=%fused_computation.28 | loop fusion | flops 2629632 | bytes 1972224 | tf_op jit(solution)/shard_map/convert_element_type | solution.py:35
  29.6 15.0 %all-to-all-done = bf16[8,40,2,2,1280]{4,3,2,1,0:T(2,128)(2,1)S(1)} async-done(((bf16[8,40,2,2,1280]{4,3,2,1,0:T(2,128)(2,1)}), bf16[8,40,2,2,1280]{4,3,2,1,0:T(2,128)(2,1)S(1)}, u32[]{:S(2)}, u32[]{:S(2)}) %all-to-all-start) | async-done | bytes 3276832 | tf_op jit(solution)/shard_map/all_to_all | solution.py:62
  44.6 5.0 %fusion.20 = f32[40,2,8,2,32]{4,2,3,1,0:T(8,128)} fusion(bf16[8,40,2,2,1280]{4,3,2,1,0:T(2,128)(2,1)S(1)} %all-to-all-done, bf16[40,16,1280]{2,1,0:T(8,128)(2,1)} %get-tuple-element.17, bf16[40,16,1280]{2,1,0:T(8,128)(2,1)} %get-tuple-element.16), kind=kOutput, calls=%fused_computation.25 | convolution fusion | flops 111411200 | bytes 6717440 | tf_op jit(solution)/shard_map/lscfk,sjk->sclfj/dot_general | solution.py:74
  49.6 0.0 copy-start.1
  49.6 0.0 copy-start
  49.6 1.5 %copy.28 = f32[40,2,8,2,32]{0,4,3,2,1:T(8,128)S(1)} copy(f32[40,2,8,2,32]{4,2,3,1,0:T(8,128)} %fusion.20) | data formatting | bytes 327680 | tf_op jit(solution)/shard_map/lscfk,sjk->sclfj/transpose | solution.py:74
  51.1 0.6 fusion.23
  51.7 0.1 copy.29
  51.9 1.0 %reshape.468 = bf16[32,2,640]{2,1,0:T(2,128)(2,1)} reshape(bf16[32,1,2,16,40]{4,3,2,1,0:T(8,128)(2,1)S(1)} %bitcast.116) | data formatting | bytes 163840
  52.9 4.0 %all-to-all-start.1 = ((bf16[32,2,640]{2,1,0:T(2,128)(2,1)}), bf16[32,2,640]{2,1,0:T(2,128)(2,1)S(1)}, u32[]{:S(2)}, u32[]{:S(2)}) async-start(bf16[32,2,640]{2,1,0:T(2,128)(2,1)} %reshape.468), calls=%async_computation.1 | async-start | bytes 163840 | tf_op jit(solution)/shard_map/all_to_all | solution.py:94
  56.9 0.6 select_multiply_fusion
  57.5 0.0 copy-done.1
  57.5 1.3 %copy.31 = bf16[64,5136]{0,1:T(8,128)(2,1)S(1)} copy(bf16[64,5136]{1,0:T(8,128)(2,1)S(1)} %copy-done.1) | data formatting | bytes 1314816 | tf_op jit(solution)/shard_map/convert_element_type | solution.py:35
  58.8 0.0 copy-done
  58.9 0.0 copy-start.9
  58.9 1.3 %copy.32 = bf16[64,5136]{0,1:T(8,128)(2,1)S(1)} copy(bf16[64,5136]{1,0:T(8,128)(2,1)S(1)} %copy-done) | data formatting | bytes 1314816 | tf_op jit(solution)/shard_map/convert_element_type | solution.py:36
  60.2 1.2 %add.119 = f32[20,5136]{1,0:T(8,128)S(1)} reshape(f32[5,4,5136]{2,1,0:T(4,128)} %get-tuple-element.21) | data formatting | bytes 821760 | tf_op jit(solution)/shard_map/add | solution.py:24
  61.3 2.0 %sub.33 = f32[20,5136]{1,0:T(8,128)} reshape(f32[5,4,5136]{2,1,0:T(4,128)} %get-tuple-element.20) | data formatting | bytes 821760 | tf_op jit(solution)/shard_map/sub | solution.py:23
  63.3 0.6 iota_compare_fusion.2
  63.9 0.5 all-to-all-done.1
  64.5 0.4 reshape.469
  64.9 0.1 copy.30
  65.0 0.3 reshape.442
  65.3 0.0 copy-done.9
  65.4 0.7 fusion.14
  66.1 0.1 squeeze.17
  66.3 0.1 squeeze.16
  66.4 0.1 maximum_bitcast_fusion.6
  66.5 0.0 copy-start.2
  66.5 2.4 %fusion.17 = f32[2,16,20,5136]{3,2,1,0:T(8,128)S(1)} fusion(bf16[64,5136]{0,1:T(8,128)(2,1)S(1)} %copy.32, bf16[64,5136]{0,1:T(8,128)(2,1)S(1)} %copy.31, bf16[1,16,20,128]{3,2,1,0:T(8,128)(2,1)S(1)} %get-tuple-element.23, bf16[1,16,20,128]{3,2,1,0:T(8,128)(2,1)S(1)} %get-tuple-element.22), kind=kOutput, calls=%fused_computation.22 | convolution fusion | flops 844193792 | bytes 14626816 | tf_op jit(solution)/shard_map/dfab,bi->dfai/dot_general | solution.py:46
  69.0 0.0 copy-done.2
  69.0 1.8 %fusion.2 = f32[16,5136]{1,0:T(8,128)S(1)} fusion(f32[2,16,20,5136]{3,2,1,0:T(8,128)S(1)} %fusion.17, f32[20,5136]{1,0:T(8,128)S(1)} %add.119, f32[20,5136]{1,0:T(8,128)S(1)} %copy-done.2), kind=kLoop, calls=%fused_computation.3 | loop fusion | flops 6491904 | bytes 14298624 | tf_op jit(solution)/shard_map/reduce_sum | solution.py:47
  70.8 0.2 reduce_sum.12
  71.0 0.2 broadcast_select_fusion.2
  71.3 10.9 %all_to_all.15 = f32[8,1,1,2,5136]{4,3,2,1,0:T(2,128)S(1)} all-to-all(f32[8,1,1,2,5136]{4,3,2,1,0:T(2,128)S(1)} %fusion.65), channel_id=1, replica_groups=mesh['wave'=4,'lev'=8] {'lev'}, dimensions={0} | all-to-all | bytes 657408 | tf_op jit(solution)/shard_map/all_to_all | solution.py:118
  82.2 0.7 copy.49
  (17 shorter events, 0.2 us)
Async XLA Ops:
  0.0 5.3 %copy-start.11 = (s32[32]{0:T(128)S(1)}, s32[32]{0:T(128)}, u32[]{:S(2)}) copy-start(s32[32]{0:T(128)} %param.9) | copy-start | bytes 388
  0.0 7.9 %copy-start.10 = (s32[32]{0:T(128)S(1)}, s32[32]{0:T(128)}, u32[]{:S(2)}) copy-start(s32[32]{0:T(128)} %param.8) | copy-start | bytes 388
  0.0 44.6 %all-to-all-start = ((bf16[8,40,2,2,1280]{4,3,2,1,0:T(2,128)(2,1)}), bf16[8,40,2,2,1280]{4,3,2,1,0:T(2,128)(2,1)S(1)}, u32[]{:S(2)}, u32[]{:S(2)}) async-start(bf16[8,40,2,2,1280]{4,3,2,1,0:T(2,128)(2,1)} %bitcast.113), calls=%async_computation | async-start | bytes 6553600 | tf_op jit(solution)/shard_map/all_to_all | solution.py:62
  22.4 4.6 %copy-start.6 = (f32[5,5136]{1,0:T(8,128)S(1)}, f32[5,5136]{1,0:T(8,128)}, u32[]{:S(2)}) copy-start(f32[5,5136]{1,0:T(8,128)} %get-tuple-element.26) | copy-start | bytes 308164
  22.4 4.6 %copy-start.7 = (f32[5,5136]{1,0:T(8,128)S(1)}, f32[5,5136]{1,0:T(8,128)}, u32[]{:S(2)}) copy-start(f32[5,5136]{1,0:T(8,128)} %get-tuple-element.27) | copy-start | bytes 308164
  22.4 4.6 %copy-start.8 = (f32[4,5136]{1,0:T(4,128)S(1)}, f32[4,5136]{1,0:T(4,128)}, u32[]{:S(2)}) copy-start(f32[4,5136]{1,0:T(4,128)} %get-tuple-element.29) | copy-start | bytes 246532
  23.4 4.8 %copy-start.3 = (f32[8,5136]{1,0:T(8,128)S(1)}, f32[8,5136]{1,0:T(8,128)}, u32[]{:S(2)}) copy-start(f32[8,5136]{1,0:T(8,128)} %get-tuple-element.37) | copy-start | bytes 493060
  23.4 4.8 %copy-start.4 = (f32[8,5136]{1,0:T(8,128)S(1)}, f32[8,5136]{1,0:T(8,128)}, u32[]{:S(2)}) copy-start(f32[8,5136]{1,0:T(8,128)} %get-tuple-element.34) | copy-start | bytes 493060
  23.4 4.8 %copy-start.5 = (f32[8,5136]{1,0:T(8,128)S(1)}, f32[8,5136]{1,0:T(8,128)}, u32[]{:S(2)}) copy-start(f32[8,5136]{1,0:T(8,128)} %get-tuple-element.35) | copy-start | bytes 493060
  49.6 7.9 %copy-start.1 = (bf16[64,5136]{1,0:T(8,128)(2,1)S(1)}, bf16[64,5136]{1,0:T(8,128)(2,1)}, u32[]{:S(2)}) copy-start(bf16[64,5136]{1,0:T(8,128)(2,1)} %get-tuple-element.18) | copy-start | bytes 1972228
  49.6 9.3 %copy-start = (bf16[64,5136]{1,0:T(8,128)(2,1)S(1)}, bf16[64,5136]{1,0:T(8,128)(2,1)}, u32[]{:S(2)}) copy-start(bf16[64,5136]{1,0:T(8,128)(2,1)} %get-tuple-element.19) | copy-start | bytes 1972228
  52.9 11.6 %all-to-all-start.1 = ((bf16[32,2,640]{2,1,0:T(2,128)(2,1)}), bf16[32,2,640]{2,1,0:T(2,128)(2,1)S(1)}, u32[]{:S(2)}, u32[]{:S(2)}) async-start(bf16[32,2,640]{2,1,0:T(2,128)(2,1)} %reshape.468), calls=%async_computation.1 | async-start | bytes 163840 | tf_op jit(solution)/shard_map/all_to_all | solution.py:94
  58.9 6.5 %copy-start.9 = (s32[1280]{0:T(1024)S(1)}, s32[1280]{0:T(1024)}, u32[]{:S(2)}) copy-start(s32[1280]{0:T(1024)} %param.7) | copy-start | bytes 15364
  66.5 2.4 %copy-start.2 = (f32[20,5136]{1,0:T(8,128)S(1)}, f32[20,5136]{1,0:T(8,128)}, u32[]{:S(2)}) copy-start(f32[20,5136]{1,0:T(8,128)} %sub.33) | copy-start | bytes 1232644
